TPU v7x, 32 devices: a whole 2x2x4 slice. The times are simulated.
32 devices in a mesh: days: 2 (over y), chan: 4 (over z), win: 4 (over x, core).
Axes of the slice: x: 2, y: 2, z: 4, core: 2. Of those that a mesh axis runs over, the one named last changes fastest.
Arguments:
- spectra: bfloat16 [2560, 32, 1024], P(('days', 'chan'), 'win'), parts along dimension 0, may hold values from -17 to 17
- pair_anchor: int32 [2048], P('chan'), may hold values from 0 to 319
- pair_offset: int32 [2048], P('chan'), may hold values from 0 to 2
- pair_partner: int32 [2048], P('chan'), may hold values from 0 to 319
- pair_count: int32 [4], P('chan'), may hold values from 1 to 512, as said below
- window_bins: int32 [64], P(('days', 'win')), parts along dimension 0, may hold values from 0 to 7
- bin_gain: float32 [8], replicated, may hold values from 0.2 to 5
Outputs:
- ref_stack: float32 [4096, 128], P(('days', 'chan')), parts along dimension 0
- restack: float32 [4096, 128], P(('days', 'chan')), parts along dimension 0
There are 2 independent parts, one for each index of `days`. A program takes and returns all parts, laid end to end along the dimension named above; an argument that names none is the same for every part. Nothing has to cross between parts.
Inputs may be any that keep to these rules, and one draw needn't show every extreme that they name: `pair_count`: each block holds from 1 to 512 live pair slots, the first ones of its slots; some block holds 512 in every draw.
All inputs are finite; a program needn't handle non-finite values.
Results may differ from a plain program's by a relative error of at most 0.0062.
Values may be sent and summed in bfloat16 or wider, within the bound.
No kernel may reach another device: no remote copies, remote signals or barrier semaphores. Data moves between devices by JAX's collectives and lax.ppermute only.
A program may use at most 128 MiB of HBM per device.

v0:
```python
import jax
import jax.numpy as jnp
from jax import lax
from jax.sharding import PartitionSpec as P

LAG = 128


EPS_POWER = 1e-05
EPS_LAG = 1e-06


def with_halo(shard, sides, width):
    for axis, dim in sides:
        peers, length = (lax.axis_size(axis), shard.shape[dim])
        up = [(i, (i + 1) % peers) for i in range(peers)]
        down = [(j, i) for i, j in up]
        last = lax.slice_in_dim(shard, length - width, length, axis=dim)
        initial = lax.slice_in_dim(shard, 0, width, axis=dim)
        before = lax.ppermute(last, axis, up)
        after = lax.ppermute(initial, axis, down)
        shard = jnp.concatenate([before, shard, after], axis=dim)
    return shard


def whiten(spectra):
    spectra_f = spectra.astype(jnp.float32)
    power_mean = jnp.mean(spectra_f * spectra_f, axis=-1, keepdims=True)
    return (spectra_f * lax.rsqrt(power_mean + EPS_POWER)).astype(jnp.bfloat16)


def lag_table(freq_count, lag_count):
    freq_ids = lax.broadcasted_iota(jnp.float32, (freq_count, lag_count), 0)
    lag_ids = lax.broadcasted_iota(jnp.float32, (freq_count, lag_count), 1) - lag_count // 2
    angles = 2.0 * jnp.pi / (2 * freq_count) * freq_ids * lag_ids
    norm_scale = 1.0 / jnp.sqrt(jnp.float32(freq_count))
    return jnp.concatenate(
        [jnp.cos(angles) * norm_scale, -jnp.sin(angles) * norm_scale], axis=0
    ).astype(jnp.bfloat16)


def cross_spectra(anchors, partners):
    half_width = anchors.shape[-1] // 2
    anchor_f = anchors.astype(jnp.float32)
    partner_f = partners.astype(jnp.float32)
    anchor_re = anchor_f[..., :half_width]
    anchor_im = anchor_f[..., half_width:]
    partner_re = partner_f[..., :half_width]
    partner_im = partner_f[..., half_width:]
    cross_re = anchor_re * partner_re + anchor_im * partner_im
    cross_im = anchor_im * partner_re - anchor_re * partner_im
    return jnp.concatenate([cross_re, cross_im], axis=-1).astype(jnp.bfloat16)


def window_gains(bins, gains):
    levels = lax.broadcasted_iota(jnp.int32, (bins.shape[0], gains.shape[0]), 1)
    return jnp.sum(jnp.where(bins[:, None] == levels, gains[None, :], jnp.float32(0.0)), axis=1)


def window_weights(lag_corr, ref_sum, window_gain):
    corr_f = lag_corr.astype(jnp.float32)
    inner_prod = jnp.mean(corr_f * ref_sum[:, None, :], axis=-1)
    corr_rms = jnp.sqrt(jnp.mean(corr_f * corr_f, axis=-1) + EPS_LAG)
    ref_rms = jnp.sqrt(jnp.mean(ref_sum * ref_sum, axis=-1) + EPS_LAG)
    coherence = inner_prod / (corr_rms * ref_rms[:, None])
    weights = window_gain[None, :] * jnp.exp(2.0 * coherence)
    numerator = jnp.sum(weights[:, :, None] * corr_f, axis=1)
    denominator = jnp.sum(weights, axis=1)
    return (numerator, denominator)


def local(spectra, pair_anchor, pair_offset, pair_partner, pair_count, window_bins, bin_gain):
    block_chans, local_wins, spec_width = spectra.shape
    pair_slots = pair_anchor.shape[0]
    white = whiten(spectra)
    nearby = with_halo(white, (("chan", 0),), block_chans)
    transform = lag_table(spec_width // 2, LAG)
    lag_count = transform.shape[1]
    block_rows = min(64, pair_slots)
    live_count = pair_count[0]
    live_steps = (live_count + block_rows - 1) // block_rows
    partner_rows = pair_offset * block_chans + pair_partner
    corr_init = jnp.zeros((pair_slots, local_wins, lag_count), jnp.bfloat16)
    running_init = jnp.zeros((pair_slots, lag_count), jnp.float32)

    def one_block(step_index, state_pair):
        corr_all, running = state_pair
        first_row = step_index * block_rows
        anchors = jnp.take(
            white, lax.dynamic_slice_in_dim(pair_anchor, first_row, block_rows), axis=0
        )
        partners = jnp.take(
            nearby, lax.dynamic_slice_in_dim(partner_rows, first_row, block_rows), axis=0
        )
        cross_spec = cross_spectra(anchors, partners)
        corr_full = jnp.dot(
            cross_spec.reshape(block_rows * local_wins, spec_width),
            transform,
            preferred_element_type=jnp.float32,
        ).reshape(block_rows, local_wins, lag_count)
        corr_all = lax.dynamic_update_slice_in_dim(
            corr_all, corr_full.astype(jnp.bfloat16), first_row, 0
        )
        partial_value = jnp.sum(corr_full, axis=1)
        running = lax.dynamic_update_slice_in_dim(running, partial_value, first_row, 0)
        return (corr_all, running)

    corr_all, running = lax.fori_loop(0, live_steps, one_block, (corr_init, running_init))
    ref_sum = lax.psum(running, "win")
    norm_scale = jnp.sqrt(jnp.float32(local_wins * lax.axis_size("win")))
    slot_ids = lax.broadcasted_iota(jnp.int32, (pair_slots,), 0)
    live_mask = (slot_ids < live_count).astype(jnp.float32)
    ref_stack = ref_sum * live_mask[:, None] / norm_scale
    window_gain = window_gains(window_bins, bin_gain)
    numerator, denominator = window_weights(corr_all, ref_sum, window_gain)
    numerator, denominator = lax.psum((numerator, denominator), "win")
    restack = norm_scale * numerator / denominator[:, None] * live_mask[:, None]
    return (ref_stack, restack)


def solution(mesh):
    in_specs = (
        P(("days", "chan"), "win", None),
        P("chan"),
        P("chan"),
        P("chan"),
        P("chan"),
        P(("days", "win")),
        P(),
    )
    out_specs = (P(("days", "chan"), None), P(("days", "chan"), None))
    return jax.shard_map(local, mesh=mesh, in_specs=in_specs, out_specs=out_specs, check_vma=False)
```

profile of v0, /device:TPU:0, one launch (start us, length us, event | category | flops | bytes accessed | tf_op | source)
XLA Modules:
  0.0 442.1 jit_solution(3069571299826950241)
XLA Ops:
  7.2 3.6 fusion.6
  11.1 5.7 %fusion.7 = bf16[320,8,1024]{2,1,0:T(8,128)(2,1)} fusion(bf16[320,8,1024]{2,1,0:T(8,128)(2,1)} %param.9, f32[320,8]{1,0:T(8,128)S(1)} %copy.12), kind=kLoop, calls=%fused_computation.24 | loop fusion | flops 7864320 | bytes 10496000 | tf_op jit(solution)/shard_map/convert_element_type | solution.py:29
  16.7 3.0 collective-permute-start
  19.7 2.0 collective-permute-start.1
  22.5 1.2 fusion.12
  23.6 0.7 pad_maximum_fusion.1
  24.4 111.6 %collective-permute-done = bf16[320,8,1024]{2,1,0:T(8,128)(2,1)} collective-permute-done((bf16[320,8,1024]{2,1,0:T(8,128)(2,1)}, bf16[320,8,1024]{2,1,0:T(8,128)(2,1)}, u32[]{:S(2)}, u32[]{:S(2)}) %collective-permute-start) | collective-permute-done | bytes 5242912 | tf_op jit(solution)/shard_map/ppermute | solution.py:20
  136.0 110.9 %collective-permute-done.1 = bf16[320,8,1024]{2,1,0:T(8,128)(2,1)} collective-permute-done((bf16[320,8,1024]{2,1,0:T(8,128)(2,1)}, bf16[320,8,1024]{2,1,0:T(8,128)(2,1)}, u32[]{:S(2)}, u32[]{:S(2)}) %collective-permute-start.1) | collective-permute-done | bytes 5242912 | tf_op jit(solution)/shard_map/ppermute | solution.py:21
  246.9 13.5 %pad_maximum_fusion = bf16[960,8,1024]{2,1,0:T(8,128)(2,1)} fusion(bf16[320,8,1024]{2,1,0:T(8,128)(2,1)} %collective-permute-done.1, bf16[320,8,1024]{2,1,0:T(8,128)(2,1)} %fusion.7, bf16[320,8,1024]{2,1,0:T(8,128)(2,1)} %collective-permute-done), kind=kLoop, calls=%fused_computation.20 | loop fusion | flops 15728640 | bytes 31457280 | tf_op jit(solution)/shard_map/concatenate | solution.py:22
  260.4 1.1 broadcast_in_dim.50
  261.6 86.5 %while.12 = (s32[]{:T(128)}, bf16[512,8,128]{2,1,0:T(8,128)(2,1)}, f32[512,128]{1,0:T(8,128)S(1)}, s32[]{:T(128)}, s32[512]{0:T(512)}, /*index=5*/bf16[320,8,102...) while((s32[]{:T(128)}, bf16[512,8,128]{2,1,0:T(8,128)(2,1)}, ...), condition=%wide.region_3.4_spmd, body=%wide.region_1.3_spmd.sunk | while | flops 140634880 | bytes 18852320 | solution.py:108
  261.6 0.8 compare_and_fusion.3
  262.4 3.1 gather_fusion.1
  265.5 0.2 select_convert_fusion.5
  265.7 6.1 %gather_fusion = bf16[64,8,1024]{2,1,0:T(8,128)(2,1)S(1)} fusion(bf16[960,8,1024]{2,1,0:T(8,128)(2,1)} %get-tuple-element.196, s32[1024]{0:T(1024)S(1)} %pad_clamp_fusion.4), kind=kCustom, calls=%fused_computation.1.clone.1 | custom fusion | bytes 2097408 | tf_op jit(solution)/shard_map/while/body/jit(_take)/gather | solution.py:92
  271.8 0.2 select_convert_fusion.4
  272.1 0.6 add_convert_fusion.2
  272.8 1.1 convert_dynamic-update-slice_fusion.2
  274.0 0.8 compare_and_fusion.3
  274.7 3.1 gather_fusion.1
  278.1 6.1 %gather_fusion = bf16[64,8,1024]{2,1,0:T(8,128)(2,1)S(1)} fusion(bf16[960,8,1024]{2,1,0:T(8,128)(2,1)} %get-tuple-element.196, s32[1024]{0:T(1024)S(1)} %pad_clamp_fusion.4), kind=kCustom, calls=%fused_computation.1.clone.1 | custom fusion | bytes 2097408 | tf_op jit(solution)/shard_map/while/body/jit(_take)/gather | solution.py:92
  284.2 0.2 select_convert_fusion.4
  284.4 0.6 add_convert_fusion.2
  285.1 1.1 convert_dynamic-update-slice_fusion.2
  286.3 0.8 compare_and_fusion.3
  287.1 3.1 gather_fusion.1
  290.2 0.2 select_convert_fusion.5
  290.4 6.1 %gather_fusion = bf16[64,8,1024]{2,1,0:T(8,128)(2,1)S(1)} fusion(bf16[960,8,1024]{2,1,0:T(8,128)(2,1)} %get-tuple-element.196, s32[1024]{0:T(1024)S(1)} %pad_clamp_fusion.4), kind=kCustom, calls=%fused_computation.1.clone.1 | custom fusion | bytes 2097408 | tf_op jit(solution)/shard_map/while/body/jit(_take)/gather | solution.py:92
  296.5 0.2 select_convert_fusion.4
  296.8 0.6 add_convert_fusion.2
  297.5 1.1 convert_dynamic-update-slice_fusion.2
  298.7 0.8 compare_and_fusion.3
  299.5 3.1 gather_fusion.1
  302.6 0.2 select_convert_fusion.5
  302.8 6.1 %gather_fusion = bf16[64,8,1024]{2,1,0:T(8,128)(2,1)S(1)} fusion(bf16[960,8,1024]{2,1,0:T(8,128)(2,1)} %get-tuple-element.196, s32[1024]{0:T(1024)S(1)} %pad_clamp_fusion.4), kind=kCustom, calls=%fused_computation.1.clone.1 | custom fusion | bytes 2097408 | tf_op jit(solution)/shard_map/while/body/jit(_take)/gather | solution.py:92
  308.9 0.2 select_convert_fusion.4
  309.1 0.6 add_convert_fusion.2
  309.8 1.1 convert_dynamic-update-slice_fusion.2
  311.0 0.8 compare_and_fusion.3
  311.8 3.1 gather_fusion.1
  315.2 6.1 %gather_fusion = bf16[64,8,1024]{2,1,0:T(8,128)(2,1)S(1)} fusion(bf16[960,8,1024]{2,1,0:T(8,128)(2,1)} %get-tuple-element.196, s32[1024]{0:T(1024)S(1)} %pad_clamp_fusion.4), kind=kCustom, calls=%fused_computation.1.clone.1 | custom fusion | bytes 2097408 | tf_op jit(solution)/shard_map/while/body/jit(_take)/gather | solution.py:92
  321.3 0.2 select_convert_fusion.4
  321.5 0.6 add_convert_fusion.2
  322.2 1.1 convert_dynamic-update-slice_fusion.2
  323.4 0.8 compare_and_fusion.3
  324.2 3.1 gather_fusion.1
  327.5 6.1 %gather_fusion = bf16[64,8,1024]{2,1,0:T(8,128)(2,1)S(1)} fusion(bf16[960,8,1024]{2,1,0:T(8,128)(2,1)} %get-tuple-element.196, s32[1024]{0:T(1024)S(1)} %pad_clamp_fusion.4), kind=kCustom, calls=%fused_computation.1.clone.1 | custom fusion | bytes 2097408 | tf_op jit(solution)/shard_map/while/body/jit(_take)/gather | solution.py:92
  333.6 0.2 select_convert_fusion.4
  333.8 0.6 add_convert_fusion.2
  334.6 1.1 convert_dynamic-update-slice_fusion.2
  335.8 0.8 compare_and_fusion.3
  336.5 3.1 gather_fusion.1
  339.9 6.1 %gather_fusion = bf16[64,8,1024]{2,1,0:T(8,128)(2,1)S(1)} fusion(bf16[960,8,1024]{2,1,0:T(8,128)(2,1)} %get-tuple-element.196, s32[1024]{0:T(1024)S(1)} %pad_clamp_fusion.4), kind=kCustom, calls=%fused_computation.1.clone.1 | custom fusion | bytes 2097408 | tf_op jit(solution)/shard_map/while/body/jit(_take)/gather | solution.py:92
  346.0 0.2 select_convert_fusion.4
  346.2 0.6 add_convert_fusion.2
  346.9 1.1 convert_dynamic-update-slice_fusion.2
  348.1 0.7 copy-done
  349.1 43.0 %all-reduce.3.cloned.1.call-done = f32[512,128]{1,0:T(8,128)} async-done(((f32[512,128]{1,0:T(8,128)}), f32[512,128]{1,0:T(8,128)}) %all-reduce.3.cloned.1.call-update) | async-done | bytes 262160 | tf_op jit(solution)/shard_map/psum | solution.py:109
  392.1 2.5 fusion.8
  394.7 1.8 multiply_reduce_fusion
  396.8 4.5 %fusion.10 = f32[512,128]{1,0:T(8,128)} fusion(bf16[512,8,128]{2,1,0:T(8,128)(2,1)} %get-tuple-element.52, f32[512,8]{1,0:T(8,128)S(1)} %copy.15), kind=kLoop, calls=%fused_computation.30 | loop fusion | flops 1507328 | bytes 1327104 | tf_op jit(solution)/shard_map/reduce_sum | solution.py:67
  401.3 5.8 %psum.23 = f32[512]{0:T(512)S(1)} all-reduce(f32[512]{0:T(512)S(1)} %get-tuple-element.77), channel_id=1, replica_groups=mesh['days'=2,'chan'=4,'win'=4] {'win'}, use_global_device_ids=true, to_apply=%region_12.13 | all-reduce | flops 512 | bytes 4096 | tf_op jit(solution)/shard_map/psum | solution.py:116
  407.1 26.4 %all-reduce.5.cloned.1.call-done = f32[512,128]{1,0:T(8,128)} async-done(((f32[512,128]{1,0:T(8,128)}), f32[512,128]{1,0:T(8,128)}) %all-reduce.5.cloned.1.call-update) | async-done | bytes 262160 | tf_op jit(solution)/shard_map/psum | solution.py:116
  433.4 1.9 divide_multiply_fusion
  (73 shorter events, 3.5 us)
Async XLA Ops:
  7.2 384.9 %all-reduce.3.cloned.1.call-start = ((), (), s32[]{:S(2)}) async-start(), calls=%async_computation | async-start | bytes 524288 | tf_op jit(solution)/shard_map/psum | solution.py:109
  11.0 13.3 %copy-start.2 = (s32[512]{0:T(512)S(1)}, s32[512]{0:T(512)}, u32[]{:S(2)}) copy-start(s32[512]{0:T(512)} %param.12) | copy-start | bytes 6148
  11.1 13.3 %copy-start.3 = (s32[512]{0:T(512)S(1)}, s32[512]{0:T(512)}, u32[]{:S(2)}) copy-start(s32[512]{0:T(512)} %param.11) | copy-start | bytes 6148
  16.7 119.3 %collective-permute-start = (bf16[320,8,1024]{2,1,0:T(8,128)(2,1)}, bf16[320,8,1024]{2,1,0:T(8,128)(2,1)}, u32[]{:S(2)}, u32[]{:S(2)}) collective-permute-start(bf16[320,8,1024]{2,1,0:T(8,128)(2,1)} %fusion.7), channel_id=1, source_target_pairs={{0,4},{4,8},{8,12},{12,0},{1,5},{5,9},{9,13},{13,1},{2,6},{6,10},{... | collective-permute-start | bytes 15728648 | tf_op jit(solution)/shard_map/ppermute | solution.py:20
  19.7 227.2 %collective-permute-start.1 = (bf16[320,8,1024]{2,1,0:T(8,128)(2,1)}, bf16[320,8,1024]{2,1,0:T(8,128)(2,1)}, u32[]{:S(2)}, u32[]{:S(2)}) collective-permute-start(bf16[320,8,1024]{2,1,0:T(8,128)(2,1)} %fusion.7), channel_id=1, source_target_pairs={{4,0},{8,4},{12,8},{0,12},{5,1},{9,5},{13,9},{1,13},{6,2},{10,6},{... | collective-permute-start | bytes 15728648 | tf_op jit(solution)/shard_map/ppermute | solution.py:21
  261.6 87.3 %copy-start.4 = (f32[8]{0:T(128)S(1)}, f32[8]{0:T(128)}, u32[]{:S(2)}) copy-start(f32[8]{0:T(128)} %param.15) | copy-start | bytes 100
  261.6 87.3 %copy-start.5 = (s32[8]{0:T(128)S(1)}, s32[8]{0:T(128)}, u32[]{:S(2)}) copy-start(s32[8]{0:T(128)} %param.14) | copy-start | bytes 100
  271.8 1.0 copy-start.1
  284.2 1.0 copy-start.1
  296.5 1.0 copy-start.1
  308.9 1.0 copy-start.1
  321.2 1.0 copy-start.1
  333.6 1.0 copy-start.1
  346.0 1.0 copy-start.1
  348.1 0.7 copy-start
  348.9 84.6 %all-reduce.5.cloned.1.call-start = ((), (), s32[]{:S(2)}) async-start(), calls=%async_computation.1 | async-start | bytes 524288 | tf_op jit(solution)/shard_map/psum | solution.py:116
Sparse Core Ops, SparseCore 0:
  349.0 43.0 all-reduce.2
  401.4 31.9 all-reduce.4
where the time goes:
time: 443 us; the launch traced here: 442 us
  waiting for transfers between devices  292 us (66%)
  local copies, waits for them, and re-layouts  67.8 us (15%)
  other arithmetic  48.4 us (11%)
  between operations  14.8 us (3%)
  matrix products  7.65 us (2%)
  blocking collectives  5.76 us (1%)
  starting transfers between devices  5.13 us (1%)
    ppermute x1, waiting for transfers between devices, with_halo(): before = lax.ppermute(last, axis, up)  112 us
    ppermute x1, waiting for transfers between devices, with_halo(): after = lax.ppermute(initial, axis, down)  111 us
    psum x1, waiting for transfers between devices, local(): ref_sum = lax.psum(running, 'win')  43 us
    gather x7, local copies, waits for them, and re-layouts, one_block(): jnp.take(nearby, lax.dynamic_slice_in_dim(partner_rows, first_row, block_...  42.6 us
    psum x1, waiting for transfers between devices, local(): numerator, denominator = lax.psum((numerator, denominator), 'win')  26.4 us
    gather x7, local copies, waits for them, and re-layouts, one_block(): jnp.take(white, lax.dynamic_slice_in_dim(pair_anchor, first_row, block_ro...  21.7 us
    concatenate x1, other arithmetic, with_halo(): shard = jnp.concatenate([before, shard, after], axis=dim)  13.5 us
  transfers between devices with their start and end apart: 4, of which 4 were waited for; matrix products, arithmetic and copies ran while one was open for 0% of the time, Pallas kernels for 0%

commit v1 on v0

--- a/solution.py
+++ b/solution.py
@@ -10,17 +10,13 @@
 EPS_LAG = 1e-06
 
 
-def with_halo(shard, sides, width):
-    for axis, dim in sides:
-        peers, length = (lax.axis_size(axis), shard.shape[dim])
-        up = [(i, (i + 1) % peers) for i in range(peers)]
-        down = [(j, i) for i, j in up]
-        last = lax.slice_in_dim(shard, length - width, length, axis=dim)
-        initial = lax.slice_in_dim(shard, 0, width, axis=dim)
-        before = lax.ppermute(last, axis, up)
-        after = lax.ppermute(initial, axis, down)
-        shard = jnp.concatenate([before, shard, after], axis=dim)
-    return shard
+def ring_neighbours(shard, axis):
+    peers = lax.axis_size(axis)
+    up = [(i, (i + 1) % peers) for i in range(peers)]
+    down = [(j, i) for i, j in up]
+    before = lax.ppermute(shard, axis, up)
+    after = lax.ppermute(shard, axis, down)
+    return before, after
 
 
 def whiten(spectra):
@@ -69,52 +65,47 @@
     return (numerator, denominator)
 
 
+def select_rows(selector, rows):
+    return jnp.einsum("sc,cwf->swf", selector, rows, preferred_element_type=jnp.float32)
+
+
 def local(spectra, pair_anchor, pair_offset, pair_partner, pair_count, window_bins, bin_gain):
     block_chans, local_wins, spec_width = spectra.shape
     pair_slots = pair_anchor.shape[0]
     white = whiten(spectra)
-    nearby = with_halo(white, (("chan", 0),), block_chans)
+    before, after = ring_neighbours(white, "chan")
     transform = lag_table(spec_width // 2, LAG)
     lag_count = transform.shape[1]
-    block_rows = min(64, pair_slots)
     live_count = pair_count[0]
-    live_steps = (live_count + block_rows - 1) // block_rows
-    partner_rows = pair_offset * block_chans + pair_partner
-    corr_init = jnp.zeros((pair_slots, local_wins, lag_count), jnp.bfloat16)
-    running_init = jnp.zeros((pair_slots, lag_count), jnp.float32)
 
-    def one_block(step_index, state_pair):
-        corr_all, running = state_pair
-        first_row = step_index * block_rows
-        anchors = jnp.take(
-            white, lax.dynamic_slice_in_dim(pair_anchor, first_row, block_rows), axis=0
-        )
-        partners = jnp.take(
-            nearby, lax.dynamic_slice_in_dim(partner_rows, first_row, block_rows), axis=0
-        )
-        cross_spec = cross_spectra(anchors, partners)
-        corr_full = jnp.dot(
-            cross_spec.reshape(block_rows * local_wins, spec_width),
-            transform,
-            preferred_element_type=jnp.float32,
-        ).reshape(block_rows, local_wins, lag_count)
-        corr_all = lax.dynamic_update_slice_in_dim(
-            corr_all, corr_full.astype(jnp.bfloat16), first_row, 0
-        )
-        partial_value = jnp.sum(corr_full, axis=1)
-        running = lax.dynamic_update_slice_in_dim(running, partial_value, first_row, 0)
-        return (corr_all, running)
+    chan_ids = lax.broadcasted_iota(jnp.int32, (pair_slots, block_chans), 1)
+    pick_anchor = (pair_anchor[:, None] == chan_ids).astype(jnp.bfloat16)
+    pick_partner = pair_partner[:, None] == chan_ids
+    offsets = pair_offset[:, None]
+    anchors = select_rows(pick_anchor, white).astype(jnp.bfloat16)
+    partners = (
+        select_rows((pick_partner & (offsets == 1)).astype(jnp.bfloat16), white)
+        + select_rows((pick_partner & (offsets == 0)).astype(jnp.bfloat16), before)
+        + select_rows((pick_partner & (offsets == 2)).astype(jnp.bfloat16), after)
+    ).astype(jnp.bfloat16)
+    cross_spec = cross_spectra(anchors, partners)
+    corr_full = jnp.dot(
+        cross_spec.reshape(pair_slots * local_wins, spec_width),
+        transform,
+        preferred_element_type=jnp.float32,
+    ).reshape(pair_slots, local_wins, lag_count)
+    corr_all = corr_full.astype(jnp.bfloat16)
+    running = jnp.sum(corr_full, axis=1)
 
-    corr_all, running = lax.fori_loop(0, live_steps, one_block, (corr_init, running_init))
     ref_sum = lax.psum(running, "win")
     norm_scale = jnp.sqrt(jnp.float32(local_wins * lax.axis_size("win")))
     slot_ids = lax.broadcasted_iota(jnp.int32, (pair_slots,), 0)
-    live_mask = (slot_ids < live_count).astype(jnp.float32)
-    ref_stack = ref_sum * live_mask[:, None] / norm_scale
+    live = slot_ids < live_count
+    ref_stack = jnp.where(live[:, None], ref_sum / norm_scale, 0.0)
     window_gain = window_gains(window_bins, bin_gain)
     numerator, denominator = window_weights(corr_all, ref_sum, window_gain)
     numerator, denominator = lax.psum((numerator, denominator), "win")
-    restack = norm_scale * numerator / denominator[:, None] * live_mask[:, None]
+    restack = jnp.where(live[:, None], norm_scale * numerator / denominator[:, None], 0.0)
     return (ref_stack, restack)
 
 

time: 443 us -> 374 us (0.84)
  local copies, waits for them, and re-layouts: 67.8 us -> 4.09 us
  matrix products: 7.65 us -> 49.1 us
  waiting for transfers between devices: 292 us -> 264 us
  other arithmetic: 48.4 us -> 31 us
    gather x14 -> x0, local copies, waits for them, and re-layouts: 64.3 us -> none  [the longest x7 42.6 us: one_block(): jnp.take(nearby, lax.dynamic_slice_in_dim(partner_rows, first_row, block_...]
    dot_general x7 -> x5, matrix products: 7.65 us -> 49.1 us  [the longest x4 45.4 us: select_rows(): jnp.einsum('sc,cwf->swf', selector, rows, preferred_element_type=jnp.floa...]
    ppermute x2, waiting for transfers between devices: 223 us -> 198 us  [the longest x1 103 us: ring_neighbours(): after = lax.ppermute(shard, axis, down)]
    concatenate x2 -> x0, other arithmetic: 14.2 us -> none  [the longest x1 13.5 us: with_halo(): shard = jnp.concatenate([before, shard, after], axis=dim)]
    another operation x8 -> x2, other arithmetic: 5.19 us -> 14.2 us
    and x7 -> x0, other arithmetic: 5.36 us -> none  [one_block(): jnp.take(nearby, lax.dynamic_slice_in_dim(partner_rows, first_row, block_...]
    reduce_sum x1, other arithmetic: 3.58 us -> 8.1 us  [whiten(): power_mean = jnp.mean(spectra_f * spectra_f, axis=-1, keepdims=True)]
  transfers between devices with their start and end apart: 4 -> 4, of which waited for: 4 -> 4; matrix products, arithmetic and copies ran while one was open for 0% -> 7% of each run, Pallas kernels for 0% -> 0%
where the time goes in v1:
time: 374 us
  waiting for transfers between devices  264 us (71%)
  matrix products  49.1 us (13%)
  other arithmetic  31 us (8%)
  between operations  14.8 us (4%)
  blocking collectives  5.73 us (2%)
  starting transfers between devices  5.43 us (1%)
  local copies, waits for them, and re-layouts  4.09 us (1%)
    ppermute x1, waiting for transfers between devices, ring_neighbours(): after = lax.ppermute(shard, axis, down)  103 us
    ppermute x1, waiting for transfers between devices, ring_neighbours(): before = lax.ppermute(shard, axis, up)  95.4 us
    dot_general x4, matrix products, select_rows(): jnp.einsum('sc,cwf->swf', selector, rows, preferred_element_type=jnp.floa...  45.4 us
    psum x1, waiting for transfers between devices, local(): ref_sum = lax.psum(running, 'win')  40 us
    psum x1, waiting for transfers between devices, local(): numerator, denominator = lax.psum((numerator, denominator), 'win')  25.6 us
    another operation x2, other arithmetic  14.2 us
    reduce_sum x1, other arithmetic, whiten(): power_mean = jnp.mean(spectra_f * spectra_f, axis=-1, keepdims=True)  8.1 us
  transfers between devices with their start and end apart: 4, of which 4 were waited for; matrix products, arithmetic and copies ran while one was open for 7% of the time, Pallas kernels for 0%

profile of v1, /device:TPU:0, one launch (start us, length us, event | category | flops | bytes accessed | tf_op | source)
XLA Modules:
  0.0 373.9 jit_solution(18302945717183395102)
XLA Ops:
  7.2 0.0 copy-start.4
  7.2 0.0 copy-start.3
  7.2 0.0 all-reduce.3.cloned.1.call-start
  7.2 0.0 copy-start
  7.2 8.1 %fusion = f32[320,8]{0,1:T(8,128)S(1)} fusion(bf16[320,8,1024]{2,1,0:T(8,128)(2,1)} %param.7), kind=kLoop, calls=%fused_computation.3 | loop fusion | flops 7861760 | bytes 5253120 | tf_op jit(solution)/shard_map/reduce_sum | solution.py:24
  15.4 0.0 copy-done
  15.4 4.2 %fusion.1 = bf16[320,8,1024]{2,0,1:T(8,128)(2,1)S(1)} fusion(f32[320,8]{0,1:T(8,128)S(1)} %add_rsqrt_fusion, bf16[320,8,1024]{2,1,0:T(8,128)(2,1)S(1)} %copy-done), kind=kLoop, calls=%fused_computation.4 | loop fusion | flops 7864320 | bytes 10496000 | tf_op jit(solution)/shard_map/convert_element_type | solution.py:25
  19.5 3.1 collective-permute-start
  22.6 2.3 collective-permute-start.1
  25.6 0.0 copy-done.4
  25.6 1.1 fusion.31
  26.7 0.0 copy-done.3
  26.7 0.0 copy-start.2
  26.7 8.2 %convert_convert_fusion = f32[512,8,1024]{2,0,1:T(8,128)} fusion(bf16[320,8,1024]{2,0,1:T(8,128)(2,1)S(1)} %fusion.1, s32[512]{0:T(512)S(1)} %copy-done.3), kind=kOutput, calls=%fused_computation.11 | convolution fusion | flops 2692907008 | bytes 22022144 | tf_op jit(solution)/shard_map/sc,cwf->swf/dot_general | solution.py:69
  35.0 0.0 copy-done.2
  35.0 8.2 %fusion.16 = f32[512,8,1024]{2,0,1:T(8,128)} fusion(bf16[320,8,1024]{2,0,1:T(8,128)(2,1)S(1)} %fusion.1, s32[512]{0:T(512)S(1)} %copy-done.2, pred[512]{0:T(512)(128)(4,1)S(1)} %get-tuple-element.17), kind=kOutput, calls=%fused_computation.26 | convolution fusion | flops 2684682240 | bytes 22022656 | tf_op jit(solution)/shard_map/sc,cwf->swf/dot_general | solution.py:69
  43.2 95.4 %collective-permute-done = bf16[320,8,1024]{2,0,1:T(8,128)(2,1)S(1)} collective-permute-done((bf16[320,8,1024]{2,0,1:T(8,128)(2,1)S(1)}, bf16[320,8,1024]{2,0,1:T(8,128)(2,1)S(1)}, u32[]{:S(2)}, u32[]{:S(2)}) %collective-permute-start) | collective-permute-done | bytes 5242912 | tf_op jit(solution)/shard_map/ppermute | solution.py:17
  138.6 8.2 %fusion.19 = f32[512,8,1024]{2,0,1:T(8,128)} fusion(bf16[320,8,1024]{2,0,1:T(8,128)(2,1)S(1)} %collective-permute-done, s32[512]{0:T(512)S(1)} %copy-done.2, pred[512]{0:T(512)(128)(4,1)S(1)} %get-tuple-element.18), kind=kOutput, calls=%fused_computation.28 | convolution fusion | flops 2684682240 | bytes 22022656 | tf_op jit(solution)/shard_map/sc,cwf->swf/dot_general | solution.py:69
  146.7 102.7 %collective-permute-done.1 = bf16[320,8,1024]{2,0,1:T(8,128)(2,1)S(1)} collective-permute-done((bf16[320,8,1024]{2,0,1:T(8,128)(2,1)S(1)}, bf16[320,8,1024]{2,0,1:T(8,128)(2,1)S(1)}, u32[]{:S(2)}, u32[]{:S(2)}) %collective-permute-start.1) | collective-permute-done | bytes 5242912 | tf_op jit(solution)/shard_map/ppermute | solution.py:18
  249.5 0.0 copy-start.1
  249.5 2.4 copy-done.1
  251.9 20.8 %fusion.6 = f32[512,8,1024]{2,0,1:T(8,128)} fusion(bf16[320,8,1024]{2,0,1:T(8,128)(2,1)} %copy-done.1, f32[512,8,1024]{2,0,1:T(8,128)} %fusion.16, f32[512,8,1024]{2,0,1:T(8,128)} %fusion.19, s32[512]{0:T(512)S(1)} %copy-done.2, pred[512]{0:T(512)(128)(4,1)S(1)} %get-tuple-element.16), kind=kOutput, calls=%fused_computation.12 | convolution fusion | flops 2701459456 | bytes 55577088 | tf_op jit(solution)/shard_map/sc,cwf->swf/dot_general | solution.py:69
  272.6 13.0 %add_convert_fusion.1 = (bf16[512,8,512]{2,0,1:T(8,128)(2,1)S(1)}, bf16[512,8,512]{2,0,1:T(8,128)(2,1)S(1)}) fusion(f32[512,8,1024]{2,0,1:T(8,128)} %fusion.6, f32[512,8,1024]{2,0,1:T(8,128)} %convert_convert_fusion), kind=kLoop, calls=%fused_computation.10 | loop fusion | flops 16777216 | bytes 41943040 | tf_op jit(solution)/shard_map/convert.2
  285.7 0.0 copy-start.5
  285.7 0.0 copy-start.6
  285.7 3.7 %fusion.39 = (f32[512,128]{0,1:T(8,128)}, bf16[512,8,128]{0,2,1:T(8,128)(2,1)S(1)}) fusion(bf16[512,128]{0,1:T(8,128)(2,1)S(1)} %get-tuple-element.15, bf16[512,128]{0,1:T(8,128)(2,1)S(1)} %get-tuple-element.14, bf16[512,8,512]{2,0,1:T(8,128)(2,1)S(1)} %get-tuple-element.11, bf16[512,8,512]{2,0,1:T(8,128)(2,1)S(1)} %get-tuple-element.10), kind=kOutput, calls=%fused_computation.63 | convolution fusion | flops 1092026368 | bytes 9961472 | tf_op jit(solution)/shard_map/dot_general | solution.py:92
  289.5 0.0 all-reduce.3.cloned.1.call-update
  289.5 0.0 all-reduce.5.cloned.1.call-start
  289.5 0.0 copy-done.5
  289.6 0.0 copy-done.6
  289.6 0.2 select_reduce_fusion
  289.7 40.0 %all-reduce.3.cloned.1.call-done = f32[512,128]{0,1:T(8,128)} async-done(((f32[512,128]{0,1:T(8,128)}), f32[512,128]{0,1:T(8,128)}) %all-reduce.3.cloned.1.call-update) | async-done | bytes 262160 | tf_op jit(solution)/shard_map/psum | solution.py:100
  329.7 1.0 multiply_reduce_fusion
  330.8 1.4 fusion.7
  332.1 0.1 fusion.38
  332.2 0.9 fusion.9
  333.1 0.0 all-reduce.5.cloned.1.call-update
  333.1 0.8 copy.15
  334.0 5.7 %psum.23 = f32[512]{0:T(512)S(1)} all-reduce(f32[512]{0:T(512)S(1)} %get-tuple-element.8), channel_id=1, replica_groups=mesh['days'=2,'chan'=4,'win'=4] {'win'}, use_global_device_ids=true, to_apply=%region_10.11 | all-reduce | flops 512 | bytes 4096 | tf_op jit(solution)/shard_map/psum | solution.py:107
  339.7 25.6 %all-reduce.5.cloned.1.call-done = f32[512,128]{0,1:T(8,128)} async-done(((f32[512,128]{0,1:T(8,128)}), f32[512,128]{0,1:T(8,128)}) %all-reduce.5.cloned.1.call-update) | async-done | bytes 262160 | tf_op jit(solution)/shard_map/psum | solution.py:107
  365.3 1.0 divide_select_fusion
  366.3 0.8 copy.16
  (6 shorter events, 0.0 us)
Async XLA Ops:
  7.2 18.4 %copy-start.4 = (s32[512]{0:T(512)S(1)}, s32[512]{0:T(512)}, u32[]{:S(2)}) copy-start(s32[512]{0:T(512)} %param.9) | copy-start | bytes 6148
  7.2 19.6 %copy-start.3 = (s32[512]{0:T(512)S(1)}, s32[512]{0:T(512)}, u32[]{:S(2)}) copy-start(s32[512]{0:T(512)} %param.8) | copy-start | bytes 6148
  7.2 322.6 %all-reduce.3.cloned.1.call-start = ((), (), s32[]{:S(2)}) async-start(), calls=%async_computation | async-start | bytes 524288 | tf_op jit(solution)/shard_map/psum | solution.py:100
  7.2 8.1 %copy-start = (bf16[320,8,1024]{2,1,0:T(8,128)(2,1)S(1)}, bf16[320,8,1024]{2,1,0:T(8,128)(2,1)}, u32[]{:S(2)}) copy-start(bf16[320,8,1024]{2,1,0:T(8,128)(2,1)} %param.7) | copy-start | bytes 15728644
  19.5 119.0 %collective-permute-start = (bf16[320,8,1024]{2,0,1:T(8,128)(2,1)S(1)}, bf16[320,8,1024]{2,0,1:T(8,128)(2,1)S(1)}, u32[]{:S(2)}, u32[]{:S(2)}) collective-permute-start(bf16[320,8,1024]{2,0,1:T(8,128)(2,1)S(1)} %fusion.1), channel_id=1, source_target_pairs={{0,4},{4,8},{8,12},{12,0},{1,5},{5,9},{9,13},{13,1},{2,6},{6,10},{... | collective-permute-start | bytes 15728648 | tf_op jit(solution)/shard_map/ppermute | solution.py:17
  22.6 226.9 %collective-permute-start.1 = (bf16[320,8,1024]{2,0,1:T(8,128)(2,1)S(1)}, bf16[320,8,1024]{2,0,1:T(8,128)(2,1)S(1)}, u32[]{:S(2)}, u32[]{:S(2)}) collective-permute-start(bf16[320,8,1024]{2,0,1:T(8,128)(2,1)S(1)} %fusion.1), channel_id=1, source_target_pairs={{4,0},{8,4},{12,8},{0,12},{5,1},{9,5},{13,9},{1,13},{6,2},{10,6},{... | collective-permute-start | bytes 15728648 | tf_op jit(solution)/shard_map/ppermute | solution.py:18
  26.7 8.2 %copy-start.2 = (s32[512]{0:T(512)S(1)}, s32[512]{0:T(512)}, u32[]{:S(2)}) copy-start(s32[512]{0:T(512)} %param.10) | copy-start | bytes 6148
  249.5 2.4 copy-start.1
  285.7 3.9 %copy-start.5 = (f32[8]{0:T(128)S(1)}, f32[8]{0:T(128)}, u32[]{:S(2)}) copy-start(f32[8]{0:T(128)} %param.13) | copy-start | bytes 100
  285.7 3.9 %copy-start.6 = (s32[8]{0:T(128)S(1)}, s32[8]{0:T(128)}, u32[]{:S(2)}) copy-start(s32[8]{0:T(128)} %param.12) | copy-start | bytes 100
  289.5 75.8 %all-reduce.5.cloned.1.call-start = ((), (), s32[]{:S(2)}) async-start(), calls=%async_computation.1 | async-start | bytes 524288 | tf_op jit(solution)/shard_map/psum | solution.py:107
Sparse Core Ops, SparseCore 0:
  289.6 40.0 all-reduce.2
  333.3 31.9 all-reduce.4
